TPU v7x, 128 devices: a whole 4x4x4 slice. The times are simulated.
128 devices in a mesh: role: 2 (over core), slab: 64 (over x, y, z).
Axes of the slice: x: 4, y: 4, z: 4, core: 2. Of those that a mesh axis runs over, the one named last changes fastest.
Arguments:
- velocity: float32 [4, 128, 128, 256], P(None, 'slab', 'role'), may hold values from -18 to 18
- basis: bfloat16 [256, 128, 128, 256], P(None, 'slab', 'role'), may hold values from -1 to 1, as said below
- mean_flow: float32 [128], replicated, may hold values from 0.2 to 2
- shear: float32 [128], replicated, may hold values from -1 to 1
Outputs:
- advanced: float32 [4, 128, 128, 256], P(None, 'slab', 'role')
- coeffs: float32 [256, 8], replicated
- rfactor: float32 [8, 8], replicated
- directions: float32 [8, 128, 128, 256], P(None, 'slab', 'role')
Inputs may be any that keep to these rules, and one draw needn't show every extreme that they name: Every column of the basis has length within a few percent of one, and distinct columns are nearly orthogonal.
All inputs are finite; a program needn't handle non-finite values.
Results may differ from a plain program's by a relative error of at most 0.00035.
The roundings to bfloat16 on the way count: a program that leaves them out, or rounds other values in their place, can miss the bound.
Values sent between devices are 32-bit elements; how exact they have to be, the bound alone decides.
No kernel may reach another device: no remote copies, remote signals or barrier semaphores. Data moves between devices by JAX's collectives and lax.ppermute only.
A program may use at most 128 MiB of HBM per device.

v0:
```python
import jax
import jax.numpy as jnp
from jax import lax
from jax.sharding import PartitionSpec as P

viscosity = 0.1
time_step = 0.4


def extended(cells, sides, width, closed):
    for axis, dim in sides:
        count = lax.axis_size(axis)
        ends = count if closed else count - 1
        head = lax.slice_in_dim(cells, 0, width, axis=dim)
        tail = lax.slice_in_dim(cells, cells.shape[dim] - width, cells.shape[dim], axis=dim)
        cells = jnp.concatenate(
            [
                lax.ppermute(tail, axis, [(i, (i + 1) % count) for i in range(ends)]),
                cells,
                lax.ppermute(head, axis, [((i + 1) % count, i) for i in range(ends)]),
            ],
            axis=dim,
        )
    return cells


def offset_slice(padded, offset, dimension, length):
    return lax.slice_in_dim(padded, 2 + offset, 2 + offset + length, axis=dimension)


def second_diff(padded, center, dimension, length):
    return (
        -offset_slice(padded, 2, dimension, length)
        + 16.0 * offset_slice(padded, 1, dimension, length)
        - 30.0 * center
        + 16.0 * offset_slice(padded, -1, dimension, length)
        - offset_slice(padded, -2, dimension, length)
    ) / 12.0


def stencil(center, xpadded, ypadded, flow_rows, shear_rows):
    nx_loc = center.shape[1]
    ny_loc = center.shape[2]
    nz_loc = center.shape[3]
    zpadded = jnp.concatenate([center[..., -2:], center, center[..., :2]], axis=3)
    first_x = (
        -offset_slice(xpadded, 2, 1, nx_loc)
        + 8.0 * offset_slice(xpadded, 1, 1, nx_loc)
        - 8.0 * offset_slice(xpadded, -1, 1, nx_loc)
        + offset_slice(xpadded, -2, 1, nx_loc)
    ) / 12.0
    laplace = (
        second_diff(xpadded, center, 1, nx_loc)
        + second_diff(ypadded, center, 2, ny_loc)
        + second_diff(zpadded, center, 3, nz_loc)
    )
    profile = flow_rows[None, None, :, None]
    result = -profile * first_x + viscosity * laplace
    shear_term = shear_rows[None, None, :, None] * center[1:2]
    return jnp.concatenate([result[:1] - shear_term, result[1:]], axis=0)


def segmented_tendency(center, flow_rows, shear_rows):
    xpadded = extended(center, (("slab", 1),), 2, True)
    ypadded = extended(center, (("role", 2),), 2, False)
    return stencil(center, xpadded, ypadded, flow_rows, shear_rows)


def on_device(velocity, basis, mean_flow, shear):
    ny_loc = velocity.shape[2]
    role_index = lax.axis_index("role")
    flow_rows = lax.dynamic_slice_in_dim(mean_flow, role_index * ny_loc, ny_loc)
    shear_rows = lax.dynamic_slice_in_dim(shear, role_index * ny_loc, ny_loc)
    tend_zero = segmented_tendency(velocity, flow_rows, shear_rows)
    segment_one = velocity + time_step * (8.0 / 15.0) * tend_zero
    tend_one = segmented_tendency(segment_one, flow_rows, shear_rows)
    advanced = segment_one + time_step * (5.0 / 12.0 * tend_one - 17.0 / 60.0 * tend_zero)
    snapshots = jnp.concatenate([segment_one, advanced], axis=0)
    flat_snaps = snapshots.reshape(snapshots.shape[0], -1)
    snaps_bf = flat_snaps.astype(jnp.bfloat16)
    basis_rows = basis.reshape(basis.shape[0], -1)
    partial_proj = jnp.einsum("km,sm->ks", basis_rows, snaps_bf, preferred_element_type=jnp.float32)
    coeffs = lax.psum(partial_proj, ("role", "slab"))
    coeffs_bf = coeffs.astype(jnp.bfloat16)
    residual = flat_snaps - jnp.einsum(
        "ks,km->sm", coeffs_bf, basis_rows, preferred_element_type=jnp.float32
    )
    local_gram = jnp.dot(residual, residual.T, precision=lax.Precision.HIGHEST)
    total_gram = lax.psum(local_gram, ("role", "slab"))
    lower_factor = jnp.linalg.cholesky(total_gram)
    directions = jax.scipy.linalg.solve_triangular(lower_factor, residual, lower=True)
    return (advanced, coeffs, lower_factor.T, directions.reshape(snapshots.shape))


def solution(mesh):
    return jax.shard_map(
        on_device,
        mesh=mesh,
        in_specs=(P(None, "slab", "role", None), P(None, "slab", "role", None), P(), P()),
        out_specs=(P(None, "slab", "role", None), P(), P(), P(None, "slab", "role", None)),
        check_vma=False,
    )
```

profile of v0, /device:TPU:1, one launch (start us, length us, event | category | flops | bytes accessed | tf_op | source)
XLA Modules:
  0.0 226.0 jit_solution(16287235402208856212)
XLA Ops:
  0.6 1.4 copy.23
  2.0 2.5 %collective-permute-start.1 = (f32[4,2,64,256]{3,0,2,1:T(4,128)S(1)}, f32[4,2,64,256]{3,0,2,1:T(4,128)S(1)}, u32[]{:S(2)}, u32[]{:S(2)}) collective-permute-start(f32[4,2,64,256]{3,0,2,1:T(4,128)S(1)} %copy.23), channel_id=1, source_target_pairs={{0,1},{1,2},{2,3},{3,4},{4,5},{5,6},{6,7},{7,8},{8,9},{9,10},{10,1... | collective-permute-start | bytes 1572872 | tf_op jit(solution)/shard_map/ppermute | solution.py:18
  4.6 6.8 %collective-permute-start = (f32[4,2,64,256]{3,0,2,1:T(4,128)S(1)}, f32[4,2,64,256]{3,0,2,1:T(4,128)S(1)}, u32[]{:S(2)}, u32[]{:S(2)}) collective-permute-start(f32[4,2,64,256]{3,0,2,1:T(4,128)S(1)} %copy.23), channel_id=1, source_target_pairs={{1,0},{2,1},{3,2},{4,3},{5,4},{6,5},{7,6},{8,7},{9,8},{10,9},{11,1... | collective-permute-start | bytes 1572872 | tf_op jit(solution)/shard_map/ppermute | solution.py:20
  11.4 2.8 %collective-permute-start.2 = (f32[4,2,2,256]{3,0,2,1:T(4,128)S(1)}, f32[4,2,2,256]{3,0,2,1:T(4,128)S(1)}, u32[]{:S(2)}, u32[]{:S(2)}) collective-permute-start(f32[4,2,2,256]{3,0,2,1:T(4,128)S(1)} %get-tuple-element.12), channel_id=1, source_target_pairs={{64,0},{65,1},{66,2},{67,3},{68,4},{69,5},{70,6},{71,7},{72,8},{73... | collective-permute-start | bytes 49160 | tf_op jit(solution)/shard_map/ppermute | solution.py:20
  14.3 1.3 collective-permute-start.3
  15.6 0.2 fusion.58
  15.8 0.7 dynamic_slice.7
  16.5 1.0 slice_multiply_fusion.3
  17.5 0.7 negate_multiply_fusion
  18.2 0.0 collective-permute-done.3
  18.2 1.5 constant_dynamic-update-slice_fusion.1
  19.7 0.0 collective-permute-done.2
  19.7 3.2 %collective-permute-done.1 = f32[4,2,64,256]{3,0,2,1:T(4,128)S(1)} collective-permute-done((f32[4,2,64,256]{3,0,2,1:T(4,128)S(1)}, f32[4,2,64,256]{3,0,2,1:T(4,128)S(1)}, u32[]{:S(2)}, u32[]{:S(2)}) %collective-permute-start.1) | collective-permute-done | bytes 524320 | tf_op jit(solution)/shard_map/ppermute | solution.py:18
  23.0 0.0 collective-permute-done
  23.0 1.9 fusion.31
  24.9 0.1 slice.185
  25.1 0.2 slice_subtract_fusion.1
  25.3 1.6 multiply_add_fusion
  26.9 0.1 collective-permute-start.5
  27.0 6.9 %collective-permute-start.4 = (f32[4,2,64,256]{3,0,2,1:T(4,128)S(1)}, f32[4,2,64,256]{3,0,2,1:T(4,128)S(1)}, u32[]{:S(2)}, u32[]{:S(2)}) collective-permute-start(f32[4,2,64,256]{3,0,2,1:T(4,128)S(1)} %multiply_add_fusion), channel_id=1, source_target_pairs={{1,0},{2,1},{3,2},{4,3},{5,4},{6,5},{7,6},{8,7},{9,8},{10,9},{11,1... | collective-permute-start | bytes 1572872 | tf_op jit(solution)/shard_map/ppermute | solution.py:20
  33.9 17.9 %copy.34 = bf16[32,8,128,256]{3,1,2,0:T(8,128)(2,1)} copy(bf16[32,8,128,256]{3,2,1,0:T(8,128)(2,1)} %bitcast.33) | data formatting | bytes 33554432
  51.7 3.7 %collective-permute-start.6 = (f32[4,2,2,256]{3,0,2,1:T(4,128)S(1)}, f32[4,2,2,256]{3,0,2,1:T(4,128)S(1)}, u32[]{:S(2)}, u32[]{:S(2)}) collective-permute-start(f32[4,2,2,256]{3,0,2,1:T(4,128)S(1)} %get-tuple-element.10), channel_id=1, source_target_pairs={{64,0},{65,1},{66,2},{67,3},{68,4},{69,5},{70,6},{71,7},{72,8},{73... | collective-permute-start | bytes 49160 | tf_op jit(solution)/shard_map/ppermute | solution.py:20
  55.4 1.5 collective-permute-start.7
  56.9 0.2 fusion.55
  57.1 0.0 collective-permute-done.6
  57.1 1.4 collective-permute-done.7
  58.5 0.0 collective-permute-done.5
  58.5 0.0 collective-permute-done.4
  58.5 2.6 %fusion.12 = f32[4,2,64,256]{3,0,2,1:T(4,128)S(1)} fusion(f32[4,2,2,256]{3,0,2,1:T(4,128)S(1)} %collective-permute-done.7, f32[4,2,64,256]{3,0,2,1:T(4,128)S(1)} %multiply_add_fusion, f32[4,2,2,256]{3,0,2,1:T(4,128)S(1)} %collective-permute-done.6, f32[4,2,64,2]{3,0,2,1:T(4,128)S(1)} %get-tuple-element.9, f32[4,2,64,2]{3,0,2,1:T(4,128)S(1)} %get-tuple-element.8, ...), kind=kLoop, calls=%fused_computation.24 | loop fusion | flops 5505024 | bytes 2138368 | tf_op jit(solution)/shard_map/add | solution.py:58
  61.1 0.2 fusion.49
  61.3 0.1 slice.200
  61.5 0.9 fusion.47
  62.4 20.8 %fusion.2 = f32[256,8]{0,1:T(8,128)S(1)} fusion(bf16[256,2,64,256]{3,2,1,0:T(8,128)(2,1)} %param.5, f32[4,2,64,256]{3,0,2,1:T(4,128)S(1)} %fusion.47, f32[4,2,64,256]{3,0,2,1:T(4,128)S(1)} %multiply_add_fusion), kind=kOutput, calls=%fused_computation.3 | convolution fusion | flops 135266304 | bytes 17833984 | tf_op jit(solution)/shard_map/km,sm->ks/dot_general | solution.py:82
  83.2 0.2 pad_maximum_fusion
  83.4 0.9 copy.28
  84.3 61.8 %psum.14 = f32[256,8]{0,1:T(8,128)S(1)} all-reduce(f32[256,8]{0,1:T(8,128)S(1)} %fusion.2), channel_id=1, replica_groups=mesh['role'=2,'slab'=64] {'role','slab'}, use_global_device_ids=true, to_apply=%region_0.0 | all-reduce | flops 2048 | bytes 16384 | tf_op jit(solution)/shard_map/psum | solution.py:83
  146.1 8.0 %convolution_subtract_fusion = f32[8,32768]{1,0:T(8,128)S(1)} fusion(f32[8,32768]{1,0:T(8,128)S(1)} %bitcast.36, bf16[256,32768]{1,0:T(8,128)(2,1)} %bitcast.34, f32[256,8]{0,1:T(8,128)S(1)} %psum.14), kind=kOutput, calls=%fused_computation | convolution fusion | flops 134481920 | bytes 18882560 | tf_op jit(solution)/shard_map/ks,km->sm/dot_general | solution.py:85
  154.1 2.3 %fusion.59 = f32[8,8]{0,1:T(8,128)S(1)} fusion(f32[8,32768]{1,0:T(8,128)S(1)} %convolution_subtract_fusion), kind=kOutput, calls=%fused_computation.104 | convolution fusion | flops 25165824 | bytes 1048832 | tf_op jit(solution)/shard_map/dot_general | solution.py:88
  156.4 63.8 %psum.15 = f32[8,8]{0,1:T(8,128)S(1)} all-reduce(f32[8,8]{0,1:T(8,128)S(1)} %fusion.59), channel_id=1, replica_groups=mesh['role'=2,'slab'=64] {'role','slab'}, use_global_device_ids=true, to_apply=%region_1.0 | all-reduce | flops 64 | bytes 512 | tf_op jit(solution)/shard_map/psum | solution.py:89
  220.2 0.1 copy.26
  220.3 0.7 cholesky.18
  221.1 0.6 compare_reduce_fusion
  221.7 0.6 select_bitcast_fusion
  222.4 0.6 custom-call.7
  223.0 1.0 fusion.50
  224.1 1.3 copy.30
  225.3 0.7 copy.29
  226.0 0.0 copy-done.1
  (9 shorter events, 0.1 us)
Async XLA Ops:
  2.0 20.9 %collective-permute-start.1 = (f32[4,2,64,256]{3,0,2,1:T(4,128)S(1)}, f32[4,2,64,256]{3,0,2,1:T(4,128)S(1)}, u32[]{:S(2)}, u32[]{:S(2)}) collective-permute-start(f32[4,2,64,256]{3,0,2,1:T(4,128)S(1)} %copy.23), channel_id=1, source_target_pairs={{0,1},{1,2},{2,3},{3,4},{4,5},{5,6},{6,7},{7,8},{8,9},{9,10},{10,1... | collective-permute-start | bytes 1572872 | tf_op jit(solution)/shard_map/ppermute | solution.py:18
  4.6 18.4 %collective-permute-start = (f32[4,2,64,256]{3,0,2,1:T(4,128)S(1)}, f32[4,2,64,256]{3,0,2,1:T(4,128)S(1)}, u32[]{:S(2)}, u32[]{:S(2)}) collective-permute-start(f32[4,2,64,256]{3,0,2,1:T(4,128)S(1)} %copy.23), channel_id=1, source_target_pairs={{1,0},{2,1},{3,2},{4,3},{5,4},{6,5},{7,6},{8,7},{9,8},{10,9},{11,1... | collective-permute-start | bytes 1572872 | tf_op jit(solution)/shard_map/ppermute | solution.py:20
  11.4 8.3 %collective-permute-start.2 = (f32[4,2,2,256]{3,0,2,1:T(4,128)S(1)}, f32[4,2,2,256]{3,0,2,1:T(4,128)S(1)}, u32[]{:S(2)}, u32[]{:S(2)}) collective-permute-start(f32[4,2,2,256]{3,0,2,1:T(4,128)S(1)} %get-tuple-element.12), channel_id=1, source_target_pairs={{64,0},{65,1},{66,2},{67,3},{68,4},{69,5},{70,6},{71,7},{72,8},{73... | collective-permute-start | bytes 49160 | tf_op jit(solution)/shard_map/ppermute | solution.py:20
  14.3 4.0 %collective-permute-start.3 = (f32[4,2,2,256]{3,0,2,1:T(4,128)S(1)}, f32[4,2,2,256]{3,0,2,1:T(4,128)S(1)}, u32[]{:S(2)}, u32[]{:S(2)}) collective-permute-start(f32[4,2,2,256]{3,0,2,1:T(4,128)S(1)} %get-tuple-element.13), channel_id=1, source_target_pairs={{0,64},{1,65},{2,66},{3,67},{4,68},{5,69},{6,70},{7,71},{8,72},{9,... | collective-permute-start | bytes 49160 | tf_op jit(solution)/shard_map/ppermute | solution.py:18
  26.9 31.6 %collective-permute-start.5 = (f32[4,2,64,256]{3,0,2,1:T(4,128)S(1)}, f32[4,2,64,256]{3,0,2,1:T(4,128)S(1)}, u32[]{:S(2)}, u32[]{:S(2)}) collective-permute-start(f32[4,2,64,256]{3,0,2,1:T(4,128)S(1)} %multiply_add_fusion), channel_id=1, source_target_pairs={{0,1},{1,2},{2,3},{3,4},{4,5},{5,6},{6,7},{7,8},{8,9},{9,10},{10,1... | collective-permute-start | bytes 1572872 | tf_op jit(solution)/shard_map/ppermute | solution.py:18
  27.0 31.5 %collective-permute-start.4 = (f32[4,2,64,256]{3,0,2,1:T(4,128)S(1)}, f32[4,2,64,256]{3,0,2,1:T(4,128)S(1)}, u32[]{:S(2)}, u32[]{:S(2)}) collective-permute-start(f32[4,2,64,256]{3,0,2,1:T(4,128)S(1)} %multiply_add_fusion), channel_id=1, source_target_pairs={{1,0},{2,1},{3,2},{4,3},{5,4},{6,5},{7,6},{8,7},{9,8},{10,9},{11,1... | collective-permute-start | bytes 1572872 | tf_op jit(solution)/shard_map/ppermute | solution.py:20
  33.8 27.6 %copy-start = (f32[4,2,64,256]{3,2,1,0:T(8,128)S(1)}, f32[4,2,64,256]{3,2,1,0:T(8,128)}, u32[]{:S(2)}) copy-start(f32[4,2,64,256]{3,2,1,0:T(8,128)} %param.4) | copy-start | bytes 1572868
  51.7 5.4 %collective-permute-start.6 = (f32[4,2,2,256]{3,0,2,1:T(4,128)S(1)}, f32[4,2,2,256]{3,0,2,1:T(4,128)S(1)}, u32[]{:S(2)}, u32[]{:S(2)}) collective-permute-start(f32[4,2,2,256]{3,0,2,1:T(4,128)S(1)} %get-tuple-element.10), channel_id=1, source_target_pairs={{64,0},{65,1},{66,2},{67,3},{68,4},{69,5},{70,6},{71,7},{72,8},{73... | collective-permute-start | bytes 49160 | tf_op jit(solution)/shard_map/ppermute | solution.py:20
  55.4 3.1 %collective-permute-start.7 = (f32[4,2,2,256]{3,0,2,1:T(4,128)S(1)}, f32[4,2,2,256]{3,0,2,1:T(4,128)S(1)}, u32[]{:S(2)}, u32[]{:S(2)}) collective-permute-start(f32[4,2,2,256]{3,0,2,1:T(4,128)S(1)} %get-tuple-element.11), channel_id=1, source_target_pairs={{0,64},{1,65},{2,66},{3,67},{4,68},{5,69},{6,70},{7,71},{8,72},{9,... | collective-permute-start | bytes 49160 | tf_op jit(solution)/shard_map/ppermute | solution.py:18
  146.1 79.9 %copy-start.1 = (f32[256,8]{0,1:T(8,128)}, f32[256,8]{0,1:T(8,128)S(1)}, u32[]{:S(2)}) copy-start(f32[256,8]{0,1:T(8,128)S(1)} %psum.14) | copy-start | bytes 24580
where the time goes:
time: 227 us; the launch traced here: 226 us
  blocking collectives  126 us (56%)
  matrix products  32.2 us (14%)
  starting transfers between devices  25.6 us (11%)
  local copies, waits for them, and re-layouts  25.1 us (11%)
  other arithmetic  12 us (5%)
  waiting for transfers between devices  4.64 us (2%)
    psum x1, blocking collectives, on_device(): total_gram = lax.psum(local_gram, ('role', 'slab'))  63.8 us
    psum x1, blocking collectives, on_device(): coeffs = lax.psum(partial_proj, ('role', 'slab'))  61.8 us
    unnamed x11, local copies, waits for them, and re-layouts  23.6 us
    dot_general x1, matrix products, on_device(): jnp.einsum('km,sm->ks', basis_rows, snaps_bf, preferred_element_type=jnp....  20.8 us
    ppermute x4, starting transfers between devices, extended(): lax.ppermute(head, axis, [((i + 1) % count, i) for i in range(ends)])  20.3 us
    dot_general x1, matrix products, on_device(): jnp.einsum('ks,km->sm', coeffs_bf, basis_rows, preferred_element_type=jnp...  8.05 us
    ppermute x4, starting transfers between devices, extended(): lax.ppermute(tail, axis, [(i, (i + 1) % count) for i in range(ends)])  5.38 us
    ppermute x4, waiting for transfers between devices, extended(): lax.ppermute(tail, axis, [(i, (i + 1) % count) for i in range(ends)])  4.63 us
  transfers between devices with their start and end apart: 8, of which 2 were waited for; matrix products, arithmetic and copies ran while one was open for 10% of the time, Pallas kernels for 0%

commit v1 on v0

--- a/solution.py
+++ b/solution.py
@@ -80,7 +80,7 @@
     snaps_bf = flat_snaps.astype(jnp.bfloat16)
     basis_rows = basis.reshape(basis.shape[0], -1)
     partial_proj = jnp.einsum("km,sm->ks", basis_rows, snaps_bf, preferred_element_type=jnp.float32)
-    coeffs = lax.psum(partial_proj, ("role", "slab"))
+    coeffs = jnp.sum(lax.all_gather(partial_proj, ("role", "slab")), axis=0)
     coeffs_bf = coeffs.astype(jnp.bfloat16)
     residual = flat_snaps - jnp.einsum(
         "ks,km->sm", coeffs_bf, basis_rows, preferred_element_type=jnp.float32

time: 227 us -> 230 us (1.013)
  blocking collectives: 126 us -> 62.4 us
  waiting for transfers between devices: 4.64 us -> 55.5 us
  between operations: 0.82 us -> 14.2 us
    psum x1 -> x0, blocking collectives: 61.8 us -> none  [on_device(): coeffs = lax.psum(partial_proj, ('role', 'slab'))]
    all_gather x0 -> x1, waiting for transfers between devices: none -> 46.9 us  [on_device(): coeffs = jnp.sum(lax.all_gather(partial_proj, ('role', 'slab')), axis=0)]
    ppermute x4, waiting for transfers between devices: 4.63 us -> 8.58 us  [extended(): lax.ppermute(tail, axis, [(i, (i + 1) % count) for i in range(ends)])]
  transfers between devices with their start and end apart: 8 -> 9, of which waited for: 2 -> 4; matrix products, arithmetic and copies ran while one was open for 10% -> 10% of each run, Pallas kernels for 0% -> 0%
where the time goes in v1:
time: 230 us; the launch traced here: 229 us
  blocking collectives  62.4 us (27%)
  waiting for transfers between devices  55.5 us (24%)
  matrix products  32.7 us (14%)
  starting transfers between devices  25.7 us (11%)
  local copies, waits for them, and re-layouts  25.3 us (11%)
  between operations  14.2 us (6%)
  other arithmetic  13.4 us (6%)
    psum x1, blocking collectives, on_device(): total_gram = lax.psum(local_gram, ('role', 'slab'))  62.4 us
    all_gather x1, waiting for transfers between devices, on_device(): coeffs = jnp.sum(lax.all_gather(partial_proj, ('role', 'slab')), axis=0)  46.9 us
    unnamed x11, local copies, waits for them, and re-layouts  23.8 us
    dot_general x1, matrix products, on_device(): jnp.einsum('km,sm->ks', basis_rows, snaps_bf, preferred_element_type=jnp....  21.3 us
    ppermute x4, starting transfers between devices, extended(): lax.ppermute(head, axis, [((i + 1) % count, i) for i in range(ends)])  20.3 us
    ppermute x4, waiting for transfers between devices, extended(): lax.ppermute(tail, axis, [(i, (i + 1) % count) for i in range(ends)])  8.58 us
    dot_general x1, matrix products, on_device(): jnp.einsum('ks,km->sm', coeffs_bf, basis_rows, preferred_element_type=jnp...  8.05 us
    ppermute x4, starting transfers between devices, extended(): lax.ppermute(tail, axis, [(i, (i + 1) % count) for i in range(ends)])  5.38 us
  transfers between devices with their start and end apart: 9, of which 4 were waited for; matrix products, arithmetic and copies ran while one was open for 10% of the time, Pallas kernels for 0%

profile of v1, /device:TPU:1, one launch (start us, length us, event | category | flops | bytes accessed | tf_op | source)
XLA Modules:
  0.0 229.2 jit_solution(15130344477520797424)
XLA Ops:
  7.2 0.0 copy-start
  7.2 0.0 all-gather.3.cloned.1.call-start
  7.2 1.4 copy.23
  8.7 2.5 %collective-permute-start.1 = (f32[4,2,64,256]{3,0,2,1:T(4,128)S(1)}, f32[4,2,64,256]{3,0,2,1:T(4,128)S(1)}, u32[]{:S(2)}, u32[]{:S(2)}) collective-permute-start(f32[4,2,64,256]{3,0,2,1:T(4,128)S(1)} %copy.23), channel_id=1, source_target_pairs={{0,1},{1,2},{2,3},{3,4},{4,5},{5,6},{6,7},{7,8},{8,9},{9,10},{10,1... | collective-permute-start | bytes 1572872 | tf_op jit(solution)/shard_map/ppermute | solution.py:18
  11.2 6.8 %collective-permute-start = (f32[4,2,64,256]{3,0,2,1:T(4,128)S(1)}, f32[4,2,64,256]{3,0,2,1:T(4,128)S(1)}, u32[]{:S(2)}, u32[]{:S(2)}) collective-permute-start(f32[4,2,64,256]{3,0,2,1:T(4,128)S(1)} %copy.23), channel_id=1, source_target_pairs={{1,0},{2,1},{3,2},{4,3},{5,4},{6,5},{7,6},{8,7},{9,8},{10,9},{11,1... | collective-permute-start | bytes 1572872 | tf_op jit(solution)/shard_map/ppermute | solution.py:20
  18.0 2.8 %collective-permute-start.2 = (f32[4,2,2,256]{3,0,2,1:T(4,128)S(1)}, f32[4,2,2,256]{3,0,2,1:T(4,128)S(1)}, u32[]{:S(2)}, u32[]{:S(2)}) collective-permute-start(f32[4,2,2,256]{3,0,2,1:T(4,128)S(1)} %get-tuple-element.12), channel_id=1, source_target_pairs={{64,0},{65,1},{66,2},{67,3},{68,4},{69,5},{70,6},{71,7},{72,8},{73... | collective-permute-start | bytes 49160 | tf_op jit(solution)/shard_map/ppermute | solution.py:20
  20.9 1.3 collective-permute-start.3
  22.2 0.2 fusion.58
  22.4 0.7 dynamic_slice.7
  23.1 1.0 slice_multiply_fusion.3
  24.1 0.7 negate_multiply_fusion
  24.9 0.0 collective-permute-done.3
  24.9 1.5 constant_dynamic-update-slice_fusion.1
  26.3 0.0 collective-permute-done.2
  26.4 3.2 %collective-permute-done.1 = f32[4,2,64,256]{3,0,2,1:T(4,128)S(1)} collective-permute-done((f32[4,2,64,256]{3,0,2,1:T(4,128)S(1)}, f32[4,2,64,256]{3,0,2,1:T(4,128)S(1)}, u32[]{:S(2)}, u32[]{:S(2)}) %collective-permute-start.1) | collective-permute-done | bytes 524320 | tf_op jit(solution)/shard_map/ppermute | solution.py:18
  29.6 1.9 fusion.31
  31.6 0.1 slice.185
  31.7 0.2 slice_subtract_fusion.1
  31.9 1.6 multiply_add_fusion
  33.5 0.1 collective-permute-start.5
  33.6 6.9 %collective-permute-start.4 = (f32[4,2,64,256]{3,0,2,1:T(4,128)S(1)}, f32[4,2,64,256]{3,0,2,1:T(4,128)S(1)}, u32[]{:S(2)}, u32[]{:S(2)}) collective-permute-start(f32[4,2,64,256]{3,0,2,1:T(4,128)S(1)} %multiply_add_fusion), channel_id=1, source_target_pairs={{1,0},{2,1},{3,2},{4,3},{5,4},{6,5},{7,6},{8,7},{9,8},{10,9},{11,1... | collective-permute-start | bytes 1572872 | tf_op jit(solution)/shard_map/ppermute | solution.py:20
  40.5 3.7 %collective-permute-start.6 = (f32[4,2,2,256]{3,0,2,1:T(4,128)S(1)}, f32[4,2,2,256]{3,0,2,1:T(4,128)S(1)}, u32[]{:S(2)}, u32[]{:S(2)}) collective-permute-start(f32[4,2,2,256]{3,0,2,1:T(4,128)S(1)} %get-tuple-element.10), channel_id=1, source_target_pairs={{64,0},{65,1},{66,2},{67,3},{68,4},{69,5},{70,6},{71,7},{72,8},{73... | collective-permute-start | bytes 49160 | tf_op jit(solution)/shard_map/ppermute | solution.py:20
  44.2 1.5 collective-permute-start.7
  45.7 0.2 fusion.55
  45.9 1.4 collective-permute-done.7
  47.3 4.0 %collective-permute-done.5 = f32[4,2,64,256]{3,0,2,1:T(4,128)S(1)} collective-permute-done((f32[4,2,64,256]{3,0,2,1:T(4,128)S(1)}, f32[4,2,64,256]{3,0,2,1:T(4,128)S(1)}, u32[]{:S(2)}, u32[]{:S(2)}) %collective-permute-start.5) | collective-permute-done | bytes 524320 | tf_op jit(solution)/shard_map/ppermute | solution.py:18
  51.2 2.6 %fusion.12 = f32[4,2,64,256]{3,0,2,1:T(4,128)S(1)} fusion(f32[4,2,2,256]{3,0,2,1:T(4,128)S(1)} %collective-permute-done.7, f32[4,2,64,256]{3,0,2,1:T(4,128)S(1)} %multiply_add_fusion, f32[4,2,2,256]{3,0,2,1:T(4,128)S(1)} %collective-permute-done.6, f32[4,2,64,2]{3,0,2,1:T(4,128)S(1)} %get-tuple-element.9, f32[4,2,64,2]{3,0,2,1:T(4,128)S(1)} %get-tuple-element.8, ...), kind=kLoop, calls=%fused_computation.24 | loop fusion | flops 5505024 | bytes 2138368 | tf_op jit(solution)/shard_map/add | solution.py:58
  53.8 0.2 fusion.49
  54.0 0.1 slice.200
  54.2 0.9 fusion.47
  55.1 21.3 %fusion.2 = f32[256,8]{0,1:T(8,128)} fusion(bf16[256,2,64,256]{3,2,1,0:T(8,128)(2,1)} %param.5, f32[4,2,64,256]{3,0,2,1:T(4,128)S(1)} %fusion.47, f32[4,2,64,256]{3,0,2,1:T(4,128)S(1)} %multiply_add_fusion), kind=kOutput, calls=%fused_computation.3 | convolution fusion | flops 135266304 | bytes 17833984 | tf_op jit(solution)/shard_map/km,sm->ks/dot_general | solution.py:82
  76.4 0.0 all-gather.3.cloned.1.call-update
  76.4 18.1 %copy.34 = bf16[32,8,128,256]{3,1,2,0:T(8,128)(2,1)} copy(bf16[32,8,128,256]{3,2,1,0:T(8,128)(2,1)} %bitcast.34) | data formatting | bytes 33554432
  94.5 0.9 copy.28
  95.4 0.2 pad_maximum_fusion
  95.6 46.9 %all-gather.3.cloned.1.call-done = f32[32768,8]{0,1:T(8,128)} async-done(((f32[256,8]{0,1:T(8,128)}), f32[32768,8]{0,1:T(8,128)}) %all-gather.3.cloned.1.call-update) | async-done | bytes 1048592 | tf_op jit(solution)/shard_map/all_gather | solution.py:83
  142.5 1.4 reduce_sum.9
  143.8 8.1 %convolution_subtract_fusion = f32[8,32768]{1,0:T(8,128)S(1)} fusion(f32[8,32768]{1,0:T(8,128)S(1)} %bitcast.37, bf16[256,32768]{1,0:T(8,128)(2,1)} %bitcast.35, f32[256,8]{0,1:T(8,128)S(1)} %reduce_sum.9), kind=kOutput, calls=%fused_computation | convolution fusion | flops 134481920 | bytes 18882560 | tf_op jit(solution)/shard_map/ks,km->sm/dot_general | solution.py:85
  151.9 2.3 %fusion.59 = f32[8,8]{0,1:T(8,128)S(1)} fusion(f32[8,32768]{1,0:T(8,128)S(1)} %convolution_subtract_fusion), kind=kOutput, calls=%fused_computation.104 | convolution fusion | flops 25165824 | bytes 1048832 | tf_op jit(solution)/shard_map/dot_general | solution.py:88
  154.2 62.4 %psum.7 = f32[8,8]{0,1:T(8,128)S(1)} all-reduce(f32[8,8]{0,1:T(8,128)S(1)} %fusion.59), channel_id=1, replica_groups=mesh['role'=2,'slab'=64] {'role','slab'}, use_global_device_ids=true, to_apply=%region_1.0 | all-reduce | flops 64 | bytes 512 | tf_op jit(solution)/shard_map/psum | solution.py:89
  216.6 0.1 copy.26
  216.7 0.7 cholesky.18
  217.4 0.6 compare_reduce_fusion
  218.1 0.6 select_bitcast_fusion
  218.8 0.6 custom-call.7
  219.4 1.0 fusion.50
  220.4 1.3 copy.30
  221.7 0.7 copy.29
  (12 shorter events, 0.1 us)
Async XLA Ops:
  7.2 47.0 %copy-start = (f32[4,2,64,256]{3,2,1,0:T(8,128)S(1)}, f32[4,2,64,256]{3,2,1,0:T(8,128)}, u32[]{:S(2)}) copy-start(f32[4,2,64,256]{3,2,1,0:T(8,128)} %param.4) | copy-start | bytes 1572868
  7.2 135.3 %all-gather.3.cloned.1.call-start = ((), (), s32[]{:S(2)}) async-start(), calls=%async_computation | async-start | bytes 1056768 | tf_op jit(solution)/shard_map/all_gather | solution.py:83
  8.7 20.9 %collective-permute-start.1 = (f32[4,2,64,256]{3,0,2,1:T(4,128)S(1)}, f32[4,2,64,256]{3,0,2,1:T(4,128)S(1)}, u32[]{:S(2)}, u32[]{:S(2)}) collective-permute-start(f32[4,2,64,256]{3,0,2,1:T(4,128)S(1)} %copy.23), channel_id=1, source_target_pairs={{0,1},{1,2},{2,3},{3,4},{4,5},{5,6},{6,7},{7,8},{8,9},{9,10},{10,1... | collective-permute-start | bytes 1572872 | tf_op jit(solution)/shard_map/ppermute | solution.py:18
  11.2 18.4 %collective-permute-start = (f32[4,2,64,256]{3,0,2,1:T(4,128)S(1)}, f32[4,2,64,256]{3,0,2,1:T(4,128)S(1)}, u32[]{:S(2)}, u32[]{:S(2)}) collective-permute-start(f32[4,2,64,256]{3,0,2,1:T(4,128)S(1)} %copy.23), channel_id=1, source_target_pairs={{1,0},{2,1},{3,2},{4,3},{5,4},{6,5},{7,6},{8,7},{9,8},{10,9},{11,1... | collective-permute-start | bytes 1572872 | tf_op jit(solution)/shard_map/ppermute | solution.py:20
  18.0 8.3 %collective-permute-start.2 = (f32[4,2,2,256]{3,0,2,1:T(4,128)S(1)}, f32[4,2,2,256]{3,0,2,1:T(4,128)S(1)}, u32[]{:S(2)}, u32[]{:S(2)}) collective-permute-start(f32[4,2,2,256]{3,0,2,1:T(4,128)S(1)} %get-tuple-element.12), channel_id=1, source_target_pairs={{64,0},{65,1},{66,2},{67,3},{68,4},{69,5},{70,6},{71,7},{72,8},{73... | collective-permute-start | bytes 49160 | tf_op jit(solution)/shard_map/ppermute | solution.py:20
  20.9 4.0 %collective-permute-start.3 = (f32[4,2,2,256]{3,0,2,1:T(4,128)S(1)}, f32[4,2,2,256]{3,0,2,1:T(4,128)S(1)}, u32[]{:S(2)}, u32[]{:S(2)}) collective-permute-start(f32[4,2,2,256]{3,0,2,1:T(4,128)S(1)} %get-tuple-element.13), channel_id=1, source_target_pairs={{0,64},{1,65},{2,66},{3,67},{4,68},{5,69},{6,70},{7,71},{8,72},{9,... | collective-permute-start | bytes 49160 | tf_op jit(solution)/shard_map/ppermute | solution.py:18
  33.5 17.7 %collective-permute-start.5 = (f32[4,2,64,256]{3,0,2,1:T(4,128)S(1)}, f32[4,2,64,256]{3,0,2,1:T(4,128)S(1)}, u32[]{:S(2)}, u32[]{:S(2)}) collective-permute-start(f32[4,2,64,256]{3,0,2,1:T(4,128)S(1)} %multiply_add_fusion), channel_id=1, source_target_pairs={{0,1},{1,2},{2,3},{3,4},{4,5},{5,6},{6,7},{7,8},{8,9},{9,10},{10,1... | collective-permute-start | bytes 1572872 | tf_op jit(solution)/shard_map/ppermute | solution.py:18
  33.6 17.6 %collective-permute-start.4 = (f32[4,2,64,256]{3,0,2,1:T(4,128)S(1)}, f32[4,2,64,256]{3,0,2,1:T(4,128)S(1)}, u32[]{:S(2)}, u32[]{:S(2)}) collective-permute-start(f32[4,2,64,256]{3,0,2,1:T(4,128)S(1)} %multiply_add_fusion), channel_id=1, source_target_pairs={{1,0},{2,1},{3,2},{4,3},{5,4},{6,5},{7,6},{8,7},{9,8},{10,9},{11,1... | collective-permute-start | bytes 1572872 | tf_op jit(solution)/shard_map/ppermute | solution.py:20
  40.5 5.4 %collective-permute-start.6 = (f32[4,2,2,256]{3,0,2,1:T(4,128)S(1)}, f32[4,2,2,256]{3,0,2,1:T(4,128)S(1)}, u32[]{:S(2)}, u32[]{:S(2)}) collective-permute-start(f32[4,2,2,256]{3,0,2,1:T(4,128)S(1)} %get-tuple-element.10), channel_id=1, source_target_pairs={{64,0},{65,1},{66,2},{67,3},{68,4},{69,5},{70,6},{71,7},{72,8},{73... | collective-permute-start | bytes 49160 | tf_op jit(solution)/shard_map/ppermute | solution.py:20
  44.2 3.1 %collective-permute-start.7 = (f32[4,2,2,256]{3,0,2,1:T(4,128)S(1)}, f32[4,2,2,256]{3,0,2,1:T(4,128)S(1)}, u32[]{:S(2)}, u32[]{:S(2)}) collective-permute-start(f32[4,2,2,256]{3,0,2,1:T(4,128)S(1)} %get-tuple-element.11), channel_id=1, source_target_pairs={{0,64},{1,65},{2,66},{3,67},{4,68},{5,69},{6,70},{7,71},{8,72},{9,... | collective-permute-start | bytes 49160 | tf_op jit(solution)/shard_map/ppermute | solution.py:18
  143.8 78.6 %copy-start.1 = (f32[256,8]{0,1:T(8,128)}, f32[256,8]{0,1:T(8,128)S(1)}, u32[]{:S(2)}) copy-start(f32[256,8]{0,1:T(8,128)S(1)} %reduce_sum.9) | copy-start | bytes 24580
Sparse Core Ops, SparseCore 0:
  76.5 65.8 all-gather.2
